TPU v7x, 512 devices: a whole 4x8x8 slice. The times are simulated.
512 devices in a mesh: row: 64 (over x, y, core), col: 8 (over z).
Axes of the slice: x: 4, y: 8, z: 8, core: 2. Of those that a mesh axis runs over, the one named last changes fastest.
Arguments:
- grad_out: bfloat16 [2048, 12288], P('row', 'col'), may hold values from -3.5 to 3.5
- pre_act: bfloat16 [2048, 24576], P('col', 'row'), may hold values from -6 to 6
- down_weight: bfloat16 [24576, 12288], P('row', 'col'), may hold values from -0.0546875 to 0.0546875
Outputs:
- grad_pre: bfloat16 [2048, 24576], P('col', 'row')
- grad_weight: bfloat16 [24576, 12288], P('row', 'col')
All inputs are finite; a program needn't handle non-finite values.
Results may differ from a plain program's by a relative error of at most 0.015.
Values may be sent and summed in bfloat16 or wider, within the bound.
No kernel may reach another device: no remote copies, remote signals or barrier semaphores. Data moves between devices by JAX's collectives and lax.ppermute only.
A program may use at most 64 MiB of HBM per device.

v0:
```python
import jax
import jax.numpy as jnp
from jax import lax
from jax.sharding import PartitionSpec as P

coef = 0.7978845608
cubic = 0.044715


def gelu_fwd(x):
    return 0.5 * x * (1.0 + jnp.tanh(coef * (x + cubic * x * x * x)))


def gelu_grad(x):
    inner = coef * (x + cubic * x * x * x)
    tangent = jnp.tanh(inner)
    return 0.5 * (1.0 + tangent) + 0.5 * x * (1.0 - tangent * tangent) * coef * (
        1.0 + 3.0 * cubic * x * x
    )


def body(grad_out, pre_act, down_weight):
    grad_all = lax.all_gather(grad_out, "row", axis=0, tiled=True)
    pre_all = lax.all_gather(pre_act, "col", axis=0, tiled=True)
    hidden = gelu_fwd(pre_all.astype(jnp.float32)).astype(jnp.bfloat16)
    grad_weight = lax.dot_general(
        hidden, grad_all, (((0,), (0,)), ((), ())), preferred_element_type=jnp.float32
    ).astype(jnp.bfloat16)
    share_rows = pre_act.shape[0]
    partial_term = lax.dot_general(
        grad_all, down_weight, (((1,), (1,)), ((), ())), preferred_element_type=jnp.float32
    )
    summed = lax.psum(partial_term.astype(jnp.bfloat16), "col").astype(jnp.float32)
    offset = lax.axis_index("col") * share_rows
    grad_hidden = lax.dynamic_slice_in_dim(summed, offset, share_rows, 0)
    grad_pre = (grad_hidden * gelu_grad(pre_act.astype(jnp.float32))).astype(jnp.bfloat16)
    return (grad_pre, grad_weight)


def solution(mesh):
    in_specs = (P("row", "col"), P("col", "row"), P("row", "col"))
    out_specs = (P("col", "row"), P("row", "col"))
    return jax.shard_map(body, mesh=mesh, in_specs=in_specs, out_specs=out_specs, check_vma=False)
```

profile of v0, /device:TPU:2, one launch (start us, length us, event | category | flops | bytes accessed | tf_op | source)
XLA Modules:
  0.0 237.7 jit_solution(11160524972806360876)
XLA Ops:
  7.2 0.0 copy-start
  7.2 0.0 all-gather.3.cloned.1.call-start
  7.2 0.7 all-gather.3.cloned.1.call-update
  7.9 0.0 all-gather.5.cloned.1.call-start
  8.0 0.7 all-gather.5.cloned.1.call-update
  8.7 0.0 all-reduce.2.cloned.1.call-start
  8.7 91.8 %all-gather.3.cloned.1.call-done = bf16[2048,1536]{1,0:T(8,128)(2,1)} async-done(((bf16[32,1536]{1,0:T(8,128)(2,1)}), bf16[2048,1536]{1,0:T(8,128)(2,1)}) %all-gather.3.cloned.1.call-update) | async-done | bytes 6291472 | tf_op jit(solution)/shard_map/all_gather | solution.py:23
  100.5 0.0 copy-done
  100.5 7.4 %convolution_convert_fusion.1 = bf16[2048,384]{1,0:T(8,128)(2,1)} fusion(bf16[2048,1536]{1,0:T(8,128)(2,1)} %all-gather.3.cloned.1.call-done, bf16[384,1536]{1,0:T(8,128)(2,1)S(1)} %copy-done), kind=kOutput, calls=%fused_computation.11 | convolution fusion | flops 2416705536 | bytes 9043968 | tf_op jit(solution)/shard_map/dot_general | solution.py:30
  107.9 0.0 all-reduce.2.cloned.1.call-update
  107.9 0.0 copy-start.1
  108.0 36.0 %all-gather.5.cloned.1.call-done = bf16[2048,384]{1,0:T(8,128)(2,1)} async-done(((bf16[256,384]{1,0:T(8,128)(2,1)}), bf16[2048,384]{1,0:T(8,128)(2,1)}) %all-gather.5.cloned.1.call-update) | async-done | bytes 1572880 | tf_op jit(solution)/shard_map/all_gather | solution.py:24
  143.9 7.0 %convolution_convert_fusion = bf16[384,1536]{1,0:T(8,128)(2,1)} fusion(bf16[2048,1536]{1,0:T(8,128)(2,1)} %all-gather.3.cloned.1.call-done, bf16[2048,384]{1,0:T(8,128)(2,1)} %all-gather.5.cloned.1.call-done), kind=kOutput, calls=%fused_computation.10 | convolution fusion | flops 2424373248 | bytes 9043968 | tf_op jit(solution)/shard_map/dot_general | solution.py:26
  150.9 78.4 %all-reduce.2.cloned.1.call-done = bf16[2048,384]{1,0:T(8,128)(2,1)} async-done(((bf16[2048,384]{1,0:T(8,128)(2,1)}), bf16[2048,384]{1,0:T(8,128)(2,1)}) %all-reduce.2.cloned.1.call-update) | async-done | bytes 1572880 | tf_op jit(solution)/shard_map/psum | solution.py:33
  229.3 0.0 copy-done.1
  229.3 1.9 fusion.17
Async XLA Ops:
  7.2 93.3 %copy-start = (bf16[384,1536]{1,0:T(8,128)(2,1)S(1)}, bf16[384,1536]{1,0:T(8,128)(2,1)}, u32[]{:S(2)}) copy-start(bf16[384,1536]{1,0:T(8,128)(2,1)} %param.5) | copy-start | bytes 3538948
  7.2 93.3 %all-gather.3.cloned.1.call-start = ((), (), s32[]{:S(2)}) async-start(), calls=%async_computation | async-start | bytes 6389760 | tf_op jit(solution)/shard_map/all_gather | solution.py:23
  7.9 136.0 %all-gather.5.cloned.1.call-start = ((), (), s32[]{:S(2)}) async-start(), calls=%async_computation.2 | async-start | bytes 1769472 | tf_op jit(solution)/shard_map/all_gather | solution.py:24
  8.7 220.7 %all-reduce.2.cloned.1.call-start = ((), (), s32[]{:S(2)}) async-start(), calls=%async_computation.1 | async-start | bytes 3145728 | tf_op jit(solution)/shard_map/psum | solution.py:33
  107.9 121.4 %copy-start.1 = (bf16[256,384]{1,0:T(8,128)(2,1)S(1)}, bf16[256,384]{1,0:T(8,128)(2,1)}, u32[]{:S(2)}) copy-start(bf16[256,384]{1,0:T(8,128)(2,1)} %param.4) | copy-start | bytes 589828
Sparse Core Ops, SparseCore 0:
  11.3 89.1 all-gather.2
  102.6 41.3 all-gather.4
  146.3 82.9 all-reduce.1
where the time goes:
time: 238 us
  waiting for transfers between devices  208 us (87%)
  matrix products  14.4 us (6%)
  between operations  13.8 us (6%)
    all_gather x1, waiting for transfers between devices, body(): grad_all = lax.all_gather(grad_out, 'row', axis=0, tiled=True)  91.8 us
    psum x1, waiting for transfers between devices, body(): lax.psum(partial_term.astype(jnp.bfloat16), 'col').astype(jnp.float32)  78.4 us
    all_gather x1, waiting for transfers between devices, body(): pre_all = lax.all_gather(pre_act, 'col', axis=0, tiled=True)  36 us
    dot_general x1, matrix products, body(): lax.dot_general(grad_all, down_weight, (((1,), (1,)), ((), ())), preferre...  7.4 us
    dot_general x1, matrix products, body(): lax.dot_general(hidden, grad_all, (((0,), (0,)), ((), ())), preferred_ele...  6.99 us
  transfers between devices with their start and end apart: 3, of which 3 were waited for; matrix products, arithmetic and copies ran while one was open for 6% of the time, Pallas kernels for 0%

commit v1 on v0

--- a/solution.py
+++ b/solution.py
@@ -30,7 +30,9 @@
     partial_term = lax.dot_general(
         grad_all, down_weight, (((1,), (1,)), ((), ())), preferred_element_type=jnp.float32
     )
-    summed = lax.psum(partial_term.astype(jnp.bfloat16), "col").astype(jnp.float32)
+    summed = jnp.sum(lax.all_gather(partial_term.astype(jnp.bfloat16), "col"), axis=0).astype(
+        jnp.float32
+    )
     offset = lax.axis_index("col") * share_rows
     grad_hidden = lax.dynamic_slice_in_dim(summed, offset, share_rows, 0)
     grad_pre = (grad_hidden * gelu_grad(pre_act.astype(jnp.float32))).astype(jnp.bfloat16)

time: 238 us -> 297 us (1.25)
  the two profiles are of different devices: /device:TPU:2 before, /device:TPU:1 now
where the time goes in v1:
time: 297 us
  waiting for transfers between devices  260 us (88%)
  matrix products  14.4 us (5%)
  between operations  13.8 us (5%)
  other arithmetic  8.35 us (3%)
    all_gather x1, waiting for transfers between devices, body(): lax.all_gather(partial_term.astype(jnp.bfloat16), 'col')  134 us
    all_gather x1, waiting for transfers between devices, body(): grad_all = lax.all_gather(grad_out, 'row', axis=0, tiled=True)  94.3 us
    all_gather x1, waiting for transfers between devices, body(): pre_all = lax.all_gather(pre_act, 'col', axis=0, tiled=True)  30.5 us
    reduce_sum x1, other arithmetic, body(): jnp.sum(lax.all_gather(partial_term.astype(jnp.bfloat16), 'col'), axis=0)  7.39 us
    dot_general x1, matrix products, body(): lax.dot_general(grad_all, down_weight, (((1,), (1,)), ((), ())), preferre...  7.38 us
    dot_general x1, matrix products, body(): lax.dot_general(hidden, grad_all, (((0,), (0,)), ((), ())), preferred_ele...  6.99 us
  transfers between devices with their start and end apart: 3, of which 3 were waited for; matrix products, arithmetic and copies ran while one was open for 5% of the time, Pallas kernels for 0%

profile of v1, /device:TPU:1, one launch (start us, length us, event | category | flops | bytes accessed | tf_op | source)
XLA Modules:
  0.0 296.6 jit_solution(3493853171715251116)
XLA Ops:
  7.2 0.0 copy-start
  7.2 0.0 all-gather.5.cloned.1.call-start
  7.2 0.7 all-gather.5.cloned.1.call-update
  7.9 0.0 all-gather.7.cloned.1.call-start
  8.0 0.7 all-gather.7.cloned.1.call-update
  8.7 0.0 all-gather.9.cloned.1.call-start
  8.7 94.3 %all-gather.5.cloned.1.call-done = bf16[2048,1536]{1,0:T(8,128)(2,1)} async-done(((bf16[32,1536]{1,0:T(8,128)(2,1)}), bf16[2048,1536]{1,0:T(8,128)(2,1)}) %all-gather.5.cloned.1.call-update) | async-done | bytes 6291472 | tf_op jit(solution)/shard_map/all_gather | solution.py:23
  103.0 0.0 copy-done
  103.0 7.4 %convolution_convert_fusion.1 = bf16[2048,384]{1,0:T(8,128)(2,1)} fusion(bf16[2048,1536]{1,0:T(8,128)(2,1)} %all-gather.5.cloned.1.call-done, bf16[384,1536]{1,0:T(8,128)(2,1)S(1)} %copy-done), kind=kOutput, calls=%fused_computation.11 | convolution fusion | flops 2416705536 | bytes 9043968 | tf_op jit(solution)/shard_map/dot_general | solution.py:30
  110.4 0.0 all-gather.9.cloned.1.call-update
  110.4 30.5 %all-gather.7.cloned.1.call-done = bf16[2048,384]{1,0:T(8,128)(2,1)} async-done(((bf16[256,384]{1,0:T(8,128)(2,1)}), bf16[2048,384]{1,0:T(8,128)(2,1)}) %all-gather.7.cloned.1.call-update) | async-done | bytes 1572880 | tf_op jit(solution)/shard_map/all_gather | solution.py:24
  140.9 7.0 %convolution_convert_fusion = bf16[384,1536]{1,0:T(8,128)(2,1)} fusion(bf16[2048,1536]{1,0:T(8,128)(2,1)} %all-gather.5.cloned.1.call-done, bf16[2048,384]{1,0:T(8,128)(2,1)} %all-gather.7.cloned.1.call-done), kind=kOutput, calls=%fused_computation.10 | convolution fusion | flops 2424373248 | bytes 9043968 | tf_op jit(solution)/shard_map/dot_general | solution.py:26
  147.9 133.8 %all-gather.9.cloned.1.call-done = bf16[16384,384]{1,0:T(8,128)(2,1)} async-done(((bf16[2048,384]{1,0:T(8,128)(2,1)}), bf16[16384,384]{1,0:T(8,128)(2,1)}) %all-gather.9.cloned.1.call-update) | async-done | bytes 12582928 | tf_op jit(solution)/shard_map/all_gather | solution.py:33
  281.7 0.0 copy-start.1
  281.7 7.4 %reduce_sum.12 = bf16[2048,384]{1,0:T(8,128)(2,1)S(1)} reduce(bf16[8,2048,384]{2,1,0:T(8,128)(2,1)} %bitcast.4, bf16[]{:T(256)} %constant.10.clone.1), dimensions={0}, to_apply=%region_0.0 | reduce | flops 5505024 | bytes 14155778 | tf_op jit(solution)/shard_map/reduce_sum | solution.py:33
  289.1 0.0 copy-done.1
  289.1 1.0 fusion.17
Async XLA Ops:
  7.2 95.8 %copy-start = (bf16[384,1536]{1,0:T(8,128)(2,1)S(1)}, bf16[384,1536]{1,0:T(8,128)(2,1)}, u32[]{:S(2)}) copy-start(bf16[384,1536]{1,0:T(8,128)(2,1)} %param.5) | copy-start | bytes 3538948
  7.2 95.8 %all-gather.5.cloned.1.call-start = ((), (), s32[]{:S(2)}) async-start(), calls=%async_computation | async-start | bytes 6389760 | tf_op jit(solution)/shard_map/all_gather | solution.py:23
  7.9 133.0 %all-gather.7.cloned.1.call-start = ((), (), s32[]{:S(2)}) async-start(), calls=%async_computation.1 | async-start | bytes 1769472 | tf_op jit(solution)/shard_map/all_gather | solution.py:24
  8.7 273.0 %all-gather.9.cloned.1.call-start = ((), (), s32[]{:S(2)}) async-start(), calls=%async_computation.2 | async-start | bytes 14155776 | tf_op jit(solution)/shard_map/all_gather | solution.py:33
  281.7 7.4 %copy-start.1 = (bf16[256,384]{1,0:T(8,128)(2,1)S(1)}, bf16[256,384]{1,0:T(8,128)(2,1)}, u32[]{:S(2)}) copy-start(bf16[256,384]{1,0:T(8,128)(2,1)} %param.4) | copy-start | bytes 589828
Sparse Core Ops, SparseCore 0:
  11.3 91.6 all-gather.4
  105.1 35.7 all-gather.6
  143.0 138.6 all-gather.8
